TPU v7x, 256 devices: a whole 4x4x8 slice. The times are simulated.
256 devices in a mesh: tm: 16 (over z, core), head: 16 (over y, x).
Axes of the slice: x: 4, y: 4, z: 8, core: 2. Of those that a mesh axis runs over, the one named last changes fastest.
Arguments:
- frames: bfloat16 [8192, 2048], P(('tm', 'head')), may hold values from -6 to 6
- log_decay: float32 [8192, 16], P('tm', 'head'), may hold values from -2 to 0, as said below
- w_query: bfloat16 [2048, 2048], P('tm', 'head'), may hold values from -0.125 to 0.125
- w_key: bfloat16 [2048, 2048], P('tm', 'head'), may hold values from -0.125 to 0.125
- w_value: bfloat16 [2048, 2048], P('tm', 'head'), may hold values from -0.125 to 0.125
- w_gate: bfloat16 [2048, 2048], P('tm', 'head'), may hold values from -0.125 to 0.125
- w_out: bfloat16 [2048, 2048], P('head', 'tm'), may hold values from -0.125 to 0.125
Outputs:
- mixed: bfloat16 [8192, 2048], P(('tm', 'head'))
Inputs may be any that keep to these rules, and one draw needn't show every extreme that they name: `log_decay`: strictly negative.
All inputs are finite; a program needn't handle non-finite values.
Results may differ from a plain program's by a relative error of at most 0.015.
Values may be sent and summed in bfloat16 or wider, within the bound.
No kernel may reach another device: no remote copies, remote signals or barrier semaphores. Data moves between devices by JAX's collectives and lax.ppermute only.
A program may use at most 64 MiB of HBM per device.

v0:
```python
import jax
import jax.numpy as jnp
from jax import lax
from jax.sharding import PartitionSpec as P

HEAD_DIM = 128
BLOCK = 512
PAD_ROWS = 8


def gather_by_exchange(part, axis):
    count = lax.axis_size(axis)
    copies = jnp.broadcast_to(part[None], (count,) + part.shape)
    return lax.all_to_all(copies, axis, 0, 0, tiled=False)


def prior_state(local_final, log_total, axis):
    heads_here = local_final.shape[0]
    high = log_total.astype(jnp.bfloat16)
    low = (log_total - high.astype(jnp.float32)).astype(jnp.bfloat16)
    extra = jnp.concatenate(
        [
            jnp.broadcast_to(high[:, None, None], (heads_here, 1, HEAD_DIM)),
            jnp.broadcast_to(low[:, None, None], (heads_here, 1, HEAD_DIM)),
            jnp.zeros((heads_here, PAD_ROWS - 2, HEAD_DIM), jnp.bfloat16),
        ],
        axis=1,
    )
    packed = jnp.concatenate([local_final.astype(jnp.bfloat16), extra], axis=1)
    gathered = gather_by_exchange(packed, axis)
    finals = gathered[:, :, :HEAD_DIM, :].astype(jnp.float32)
    totals = gathered[:, :, HEAD_DIM, 0].astype(jnp.float32) + gathered[
        :, :, HEAD_DIM + 1, 0
    ].astype(jnp.float32)
    count = gathered.shape[0]
    mine = lax.axis_index(axis)
    order = jnp.arange(count, dtype=jnp.int32)
    between = (order[:, None] < order[None, :]) & (order[None, :] < mine)
    exponent = jnp.sum(jnp.where(between[:, :, None], totals[None, :, :], 0.0), axis=1)
    weight = jnp.where((order < mine)[:, None], jnp.exp(exponent), 0.0)
    return jnp.sum(weight[:, :, None, None] * finals, axis=0)


def shards(frames, log_decay, w_query, w_key, w_value, w_gate, w_out):
    head_width = w_query.shape[1]
    blocks = [w_query, w_key, w_value, w_gate, w_out]
    width = sum((block.shape[1] for block in blocks))
    column = jnp.arange(width)[None, :]
    packed = jnp.pad(blocks[-1], ((0, 0), (width - head_width, 0)))
    for start, block in reversed(list(zip(range(0, width, head_width), blocks))[:-1]):
        padded = jnp.pad(block, ((0, 0), (start, width - start - head_width)))
        packed = jnp.where(column < start + head_width, padded, packed)
    stacked = lax.all_gather(packed, "tm", axis=0, tiled=True)
    joined = stacked[:, : 4 * head_width]
    out_blocks = stacked[:, 4 * head_width :].reshape(-1, head_width, w_out.shape[1])
    frames_here = gather_by_exchange(frames, "head").reshape(-1, frames.shape[1])
    projected = jnp.dot(frames_here, joined, preferred_element_type=jnp.float32)
    local_len = projected.shape[0]
    heads_here = head_width // HEAD_DIM
    block_count = local_len // BLOCK
    query_blocks = (
        projected[:, :head_width]
        .astype(jnp.bfloat16)
        .reshape(block_count, BLOCK, heads_here, HEAD_DIM)
    )
    key_blocks = (
        projected[:, head_width : 2 * head_width]
        .astype(jnp.bfloat16)
        .reshape(block_count, BLOCK, heads_here, HEAD_DIM)
    )
    value_blocks = (
        projected[:, 2 * head_width : 3 * head_width]
        .astype(jnp.bfloat16)
        .reshape(block_count, BLOCK, heads_here, HEAD_DIM)
    )
    gate_all = projected[:, 3 * head_width :]
    running_blocks = jnp.cumsum(log_decay.reshape(block_count, BLOCK, heads_here), axis=1)
    slice_ordinal = jnp.arange(BLOCK, dtype=jnp.int32)
    causal = slice_ordinal[:, None] >= slice_ordinal[None, :]

    def local_step(carry_state, inputs):
        query_block, key_block, value_block, running = inputs
        gaps = running.T[:, :, None] - running.T[:, None, :]
        decay = jnp.exp(jnp.where(causal[None], gaps, -jnp.inf))
        scores = jnp.einsum(
            "thd,shd->hts", query_block, key_block, preferred_element_type=jnp.float32
        )
        weights = (scores * decay).astype(jnp.bfloat16)
        intra = jnp.einsum("hts,shd->thd", weights, value_block, preferred_element_type=jnp.float32)
        scaled = (
            key_block.astype(jnp.float32) * jnp.exp(running[-1][None, :] - running)[:, :, None]
        ).astype(jnp.bfloat16)
        update = jnp.einsum("shd,she->hde", scaled, value_block, preferred_element_type=jnp.float32)
        next_state = jnp.exp(running[-1])[:, None, None] * carry_state + update
        return (next_state, (intra, carry_state))

    zero_state = jnp.zeros((heads_here, HEAD_DIM, HEAD_DIM), jnp.float32)
    local_final, (intra_all, local_starts) = lax.scan(
        local_step, zero_state, (query_blocks, key_blocks, value_blocks, running_blocks)
    )
    prior = prior_state(local_final, jnp.sum(log_decay, axis=0), "tm")
    block_logs = running_blocks[:, -1, :]
    before = jnp.cumsum(block_logs, axis=0) - block_logs
    start_states = jnp.exp(before)[:, :, None, None] * prior[None] + local_starts
    lifted = query_blocks.astype(jnp.float32) * jnp.exp(running_blocks)[..., None]
    inter = jnp.einsum("cthd,chde->cthe", lifted, start_states, precision=lax.Precision.HIGHEST)
    retained = (intra_all + inter).reshape(local_len, heads_here, HEAD_DIM)
    center = jnp.mean(retained, axis=-1, keepdims=True)
    spread = jnp.mean((retained - center) ** 2, axis=-1, keepdims=True)
    normed = (retained - center) / jnp.sqrt(spread + 1e-05)
    gated = (
        (jax.nn.silu(gate_all.reshape(local_len, heads_here, HEAD_DIM)) * normed)
        .astype(jnp.bfloat16)
        .reshape(local_len, head_width)
    )
    heads = lax.axis_size("head")
    side = int(round(heads**0.5))
    me = lax.axis_index("head")
    row, col = (me // side, me % side)
    rows_mine = out_blocks
    ring_order = sorted(range(1, side), key=lambda shift: -min(shift, side - shift))
    by_owner = gated.reshape(side, side, local_len // heads, head_width)
    units = lax.axis_size("tm")
    half = rows_mine.shape[0] // 2
    parity = lax.axis_index("tm") % 2
    own_half = lax.dynamic_slice_in_dim(rows_mine, parity * half, half, axis=0)
    pieces = [lax.dynamic_index_in_dim(by_owner, col, axis=1, keepdims=False)]
    fetched = []
    for shift in ring_order:
        across = [(h, h // side * side + (h % side + shift) % side) for h in range(heads)]
        piece = lax.dynamic_index_in_dim(by_owner, (col + shift) % side, axis=1, keepdims=False)
        pieces.append(lax.ppermute(piece, "head", across))
        fetched.append(lax.ppermute(own_half, "head", across))
    fetched = jnp.stack(fetched)
    swapped = lax.ppermute(fetched, "tm", [(t, t ^ 1) for t in range(units)])
    first = jnp.where(parity == 0, fetched, swapped)
    second = jnp.where(parity == 0, swapped, fetched)
    remote = jnp.concatenate([first, second], axis=1)
    weights_in = [rows_mine] + [remote[s] for s in range(side - 1)]
    partial = jnp.einsum(
        "syfr,skrc->yfkc",
        jnp.stack(pieces),
        jnp.stack(weights_in),
        preferred_element_type=jnp.float32,
    ).astype(jnp.bfloat16)
    partial = partial.reshape(side, local_len // heads, -1)
    total = lax.dynamic_index_in_dim(partial, row, axis=0, keepdims=False).astype(jnp.float32)
    for shift in ring_order:
        down = [(h, (h // side + shift) % side * side + h % side) for h in range(heads)]
        piece = lax.dynamic_index_in_dim(partial, (row + shift) % side, axis=0, keepdims=False)
        total = total + lax.ppermute(piece, "head", down).astype(jnp.float32)
    return total.astype(jnp.bfloat16)


def solution(mesh):
    return jax.shard_map(
        shards,
        mesh=mesh,
        in_specs=(
            P(("tm", "head"), None),
            P("tm", "head"),
            P("tm", "head"),
            P("tm", "head"),
            P("tm", "head"),
            P("tm", "head"),
            P("head", "tm"),
        ),
        out_specs=P(("tm", "head"), None),
        check_vma=False,
    )
```

profile of v0, /device:TPU:6, one launch (start us, length us, event | category | flops | bytes accessed | tf_op | source)
XLA Modules:
  0.0 110.7 jit_solution(12447846987612990103)
XLA Ops:
  6.5 1.6 %select_select_fusion = bf16[128,640]{1,0:T(8,128)(2,1)} fusion(bf16[128,128]{1,0:T(8,128)(2,1)} %param.13, bf16[128,128]{1,0:T(8,128)(2,1)} %param.12, bf16[128,128]{1,0:T(8,128)(2,1)} %param.11, bf16[128,128]{1,0:T(8,128)(2,1)} %param.10, bf16[128,128]{1,0:T(8,128)(2,1)} %param.9, pred[640]{0:T(1024)(128)(4,1)S(1)} %get-tuple-element.47, ...), kind=kLoop, calls=%fused_computation.47 | loop fusion | flops 327680 | bytes 330240 | tf_op jit(solution)/shard_map/jit(_where)/select_n | solution.py:52
  8.1 2.5 %broadcast_in_dim.113 = bf16[16,32,2048]{2,1,0:T(8,128)(2,1)} broadcast(bf16[32,2048]{1,0:T(8,128)(2,1)} %param.7), dimensions={1,2} | broadcast | bytes 2228224 | tf_op jit(solution)/shard_map/broadcast_in_dim | solution.py:13
  10.6 7.6 %all-to-all-start = ((bf16[16,32,2048]{2,1,0:T(8,128)(2,1)}), bf16[16,32,2048]{2,1,0:T(8,128)(2,1)S(1)}, u32[]{:S(2)}, u32[]{:S(2)}) async-start(bf16[16,32,2048]{2,1,0:T(8,128)(2,1)} %broadcast_in_dim.113), calls=%async_computation | async-start | bytes 4194304 | tf_op jit(solution)/shard_map/all_to_all | solution.py:14
  18.2 0.7 reduce_sum.47
  18.8 0.3 reduce-window.6
  19.1 0.2 slice_reduce_fusion
  19.3 0.2 reduce-window.9
  19.6 0.6 slice.69
  20.1 0.6 slice.68
  23.6 22.9 %all-to-all-done = bf16[16,32,2048]{2,1,0:T(8,128)(2,1)S(1)} async-done(((bf16[16,32,2048]{2,1,0:T(8,128)(2,1)}), bf16[16,32,2048]{2,1,0:T(8,128)(2,1)S(1)}, u32[]{:S(2)}, u32[]{:S(2)}) %all-to-all-start) | async-done | bytes 2097184 | tf_op jit(solution)/shard_map/all_to_all | solution.py:14
  46.4 6.1 %all-gather.2.cloned.1.call-done = bf16[2048,640]{1,0:T(8,128)(2,1)} async-done(((bf16[128,640]{1,0:T(8,128)(2,1)}), bf16[2048,640]{1,0:T(8,128)(2,1)}) %all-gather.2.cloned.1.call-update) | async-done | bytes 2621456 | tf_op jit(solution)/shard_map/all_gather | solution.py:53
  52.6 3.8 %fusion.58 = (bf16[512,512]{1,0:T(8,128)(2,1)S(1)}, f32[512,512]{1,0:T(8,128)}) fusion(bf16[512,2048]{1,0:T(8,128)(2,1)S(1)} %bitcast.110, bf16[2048,640]{1,0:T(8,128)(2,1)} %all-gather.2.cloned.1.call-done), kind=kOutput, calls=%fused_computation.95 | convolution fusion | flops 1074003968 | bytes 5767168 | tf_op jit(solution)/shard_map/dot_general | solution.py:57
  56.4 0.3 fusion.18
  56.8 0.1 maximum_bitcast_fusion.10
  56.9 0.9 broadcast_in_dim.122
  57.8 4.0 %all-to-all-start.1 = ((bf16[16,1,136,128]{3,2,1,0:T(8,128)(2,1)}), bf16[16,1,136,128]{3,2,1,0:T(8,128)(2,1)S(1)}, u32[]{:S(2)}, u32[]{:S(2)}) async-start(bf16[16,1,136,128]{3,2,1,0:T(8,128)(2,1)} %broadcast_in_dim.122), calls=%async_computation.1 | async-start | bytes 1114112 | tf_op jit(solution)/shard_map/all_to_all | solution.py:14
  62.0 0.6 slice.67
  62.6 0.6 slice.66
  64.4 1.1 slice.73
  65.6 1.5 %collective-permute-start.3 = (bf16[8,128,128]{2,1,0:T(8,128)(2,1)S(1)}, bf16[8,128,128]{2,1,0:T(8,128)(2,1)S(1)}, u32[]{:S(2)}, u32[]{:S(2)}) collective-permute-start(bf16[8,128,128]{2,1,0:T(8,128)(2,1)S(1)} %constant_dynamic-slice_fusion), channel_id=1, source_target_pairs={{0,2},{1,3},{2,0},{3,1},{4,6},{5,7},{6,4},{7,5},{8,10},{9,11},{10,... | collective-permute-start | bytes 786440 | tf_op jit(solution)/shard_map/ppermute | solution.py:133
  67.1 2.4 %collective-permute-start.4 = (bf16[8,128,128]{2,1,0:T(8,128)(2,1)S(1)}, bf16[8,128,128]{2,1,0:T(8,128)(2,1)S(1)}, u32[]{:S(2)}, u32[]{:S(2)}) collective-permute-start(bf16[8,128,128]{2,1,0:T(8,128)(2,1)S(1)} %constant_dynamic-slice_fusion), channel_id=1, source_target_pairs={{0,1},{1,2},{2,3},{3,0},{4,5},{5,6},{6,7},{7,4},{8,9},{9,10},{10,1... | collective-permute-start | bytes 786440 | tf_op jit(solution)/shard_map/ppermute | solution.py:133
  69.5 1.2 %fusion.15 = f32[1,512,1,128]{3,1,2,0:T(8,128)} fusion(f32[512]{0:T(512)S(1)} %get-tuple-element.22, bf16[512,512]{1,0:T(8,128)(2,1)S(1)} %get-tuple-element.43), kind=kOutput, calls=%fused_computation.16 | convolution fusion | flops 135528448 | bytes 659456 | tf_op jit(solution)/shard_map/while/body/eval_jaxpr/hts,shd->thd/dot_general | solution.py:89
  70.7 5.6 %collective-permute-done.3 = bf16[8,128,128]{2,1,0:T(8,128)(2,1)S(1)} collective-permute-done((bf16[8,128,128]{2,1,0:T(8,128)(2,1)S(1)}, bf16[8,128,128]{2,1,0:T(8,128)(2,1)S(1)}, u32[]{:S(2)}, u32[]{:S(2)}) %collective-permute-start.3) | collective-permute-done | bytes 262176 | tf_op jit(solution)/shard_map/ppermute | solution.py:133
  76.3 4.1 %collective-permute-done.4 = bf16[8,128,128]{2,1,0:T(8,128)(2,1)S(1)} collective-permute-done((bf16[8,128,128]{2,1,0:T(8,128)(2,1)S(1)}, bf16[8,128,128]{2,1,0:T(8,128)(2,1)S(1)}, u32[]{:S(2)}, u32[]{:S(2)}) %collective-permute-start.4) | collective-permute-done | bytes 262176 | tf_op jit(solution)/shard_map/ppermute | solution.py:133
  80.5 0.8 collective-permute-done.5
  81.3 0.1 pad_maximum_fusion
  81.3 0.1 collective-permute-start.6
  81.5 0.2 fusion.55
  81.7 0.1 select_reduce_fusion
  81.8 0.2 multiply_reduce_fusion
  82.0 1.5 %fusion.59 = (f32[512]{0:T(512)S(1)}, f32[1,512,1,128]{3,1,2,0:T(8,128)S(1)}) fusion(f32[1,512,1,128]{3,1,2,0:T(8,128)} %fusion.15, f32[512]{0:T(512)S(1)} %exp.53, bf16[512,512]{1,0:T(8,128)(2,1)} %copy-done, f32[128,128]{1,0:T(8,128)S(1)} %multiply_reduce_fusion, f32[]{:T(128)} %bitcast.11), kind=kOutput, calls=%fused_computation.96 | convolution fusion | flops 100941312 | bytes 725504 | tf_op jit(solution)/shard_map/cthd,chde->cthe/dot_general | solution.py:106
  83.5 0.2 fusion.29
  83.8 1.2 %fusion.32 = bf16[512,128]{1,0:T(8,128)(2,1)S(1)} fusion(f32[1,512,1,128]{3,1,2,0:T(8,128)S(1)} %get-tuple-element.46, f32[512,512]{1,0:T(8,128)} %get-tuple-element.44, f32[512]{0:T(512)S(1)} %add_sqrt_fusion, f32[512]{0:T(512)S(1)} %broadcast_multiply_fusion), kind=kLoop, calls=%fused_computation.43 | loop fusion | flops 524288 | bytes 659456 | tf_op jit(solution)/shard_map/convert_element_type | solution.py:113
  85.0 1.9 %collective-permute-start = (bf16[4,32,128]{2,1,0:T(8,128)(2,1)S(1)}, bf16[4,32,128]{2,1,0:T(8,128)(2,1)S(1)}, u32[]{:S(2)}, u32[]{:S(2)}) collective-permute-start(bf16[4,32,128]{2,1,0:T(8,128)(2,1)S(1)} %get-tuple-element.42), channel_id=1, source_target_pairs={{0,2},{1,3},{2,0},{3,1},{4,6},{5,7},{6,4},{7,5},{8,10},{9,11},{10,... | collective-permute-start | bytes 98312 | tf_op jit(solution)/shard_map/ppermute | solution.py:132
  86.9 1.8 %collective-permute-start.1 = (bf16[4,32,128]{2,1,0:T(8,128)(2,1)S(1)}, bf16[4,32,128]{2,1,0:T(8,128)(2,1)S(1)}, u32[]{:S(2)}, u32[]{:S(2)}) collective-permute-start(bf16[4,32,128]{2,1,0:T(8,128)(2,1)S(1)} %get-tuple-element.41), channel_id=1, source_target_pairs={{0,1},{1,2},{2,3},{3,0},{4,5},{5,6},{6,7},{7,4},{8,9},{9,10},{10,1... | collective-permute-start | bytes 98312 | tf_op jit(solution)/shard_map/ppermute | solution.py:132
  88.7 0.2 collective-permute-start.2
  88.9 0.1 broadcast_select_fusion.1
  89.0 1.5 %collective-permute-done = bf16[4,32,128]{2,1,0:T(8,128)(2,1)S(1)} collective-permute-done((bf16[4,32,128]{2,1,0:T(8,128)(2,1)S(1)}, bf16[4,32,128]{2,1,0:T(8,128)(2,1)S(1)}, u32[]{:S(2)}, u32[]{:S(2)}) %collective-permute-start) | collective-permute-done | bytes 32800 | tf_op jit(solution)/shard_map/ppermute | solution.py:132
  90.5 0.3 collective-permute-done.1
  90.8 3.0 %collective-permute-done.2 = bf16[4,32,128]{2,1,0:T(8,128)(2,1)S(1)} collective-permute-done((bf16[4,32,128]{2,1,0:T(8,128)(2,1)S(1)}, bf16[4,32,128]{2,1,0:T(8,128)(2,1)S(1)}, u32[]{:S(2)}, u32[]{:S(2)}) %collective-permute-start.2) | collective-permute-done | bytes 32800 | tf_op jit(solution)/shard_map/ppermute | solution.py:132
  93.8 0.5 fusion.13
  94.2 0.1 copy.38
  94.4 2.2 %collective-permute-start.7 = (bf16[32,2048]{1,0:T(8,128)(2,1)S(1)}, bf16[32,2048]{1,0:T(8,128)(2,1)S(1)}, u32[]{:S(2)}, u32[]{:S(2)}) collective-permute-start(bf16[32,2048]{1,0:T(8,128)(2,1)S(1)} %get-tuple-element.25), channel_id=1, source_target_pairs={{0,8},{1,9},{2,10},{3,11},{4,12},{5,13},{6,14},{7,15},{8,0},{9,1},... | collective-permute-start | bytes 393224 | tf_op jit(solution)/shard_map/ppermute | solution.py:151
  96.6 0.6 collective-permute-start.8
  97.2 2.6 %collective-permute-start.9 = (bf16[32,2048]{1,0:T(8,128)(2,1)S(1)}, bf16[32,2048]{1,0:T(8,128)(2,1)S(1)}, u32[]{:S(2)}, u32[]{:S(2)}) collective-permute-start(bf16[32,2048]{1,0:T(8,128)(2,1)S(1)} %get-tuple-element.26), channel_id=1, source_target_pairs={{0,12},{1,13},{2,14},{3,15},{4,0},{5,1},{6,2},{7,3},{8,4},{9,5},{1... | collective-permute-start | bytes 393224 | tf_op jit(solution)/shard_map/ppermute | solution.py:151
  99.8 1.9 %collective-permute-done.7 = bf16[32,2048]{1,0:T(8,128)(2,1)S(1)} collective-permute-done((bf16[32,2048]{1,0:T(8,128)(2,1)S(1)}, bf16[32,2048]{1,0:T(8,128)(2,1)S(1)}, u32[]{:S(2)}, u32[]{:S(2)}) %collective-permute-start.7) | collective-permute-done | bytes 131104 | tf_op jit(solution)/shard_map/ppermute | solution.py:151
  101.7 1.4 %collective-permute-done.8 = bf16[32,2048]{1,0:T(8,128)(2,1)S(1)} collective-permute-done((bf16[32,2048]{1,0:T(8,128)(2,1)S(1)}, bf16[32,2048]{1,0:T(8,128)(2,1)S(1)}, u32[]{:S(2)}, u32[]{:S(2)}) %collective-permute-start.8) | collective-permute-done | bytes 131104 | tf_op jit(solution)/shard_map/ppermute | solution.py:151
  103.1 0.7 fusion.27
  (27 shorter events, 0.5 us)
Async XLA Ops:
  6.5 46.1 %all-gather.2.cloned.1.call-start = ((), (), s32[]{:S(2)}) async-start(), calls=%async_computation.2 | async-start | bytes 2785280 | tf_op jit(solution)/shard_map/all_gather | solution.py:53
  10.6 7.6 %copy-start.1 = (f32[512,1]{0,1:T(1,128)S(1)}, f32[512,1]{0,1:T(1,128)}, u32[]{:S(2)}) copy-start(f32[512,1]{0,1:T(1,128)} %param.8) | copy-start | bytes 6148
  10.6 35.8 %all-to-all-start = ((bf16[16,32,2048]{2,1,0:T(8,128)(2,1)}), bf16[16,32,2048]{2,1,0:T(8,128)(2,1)S(1)}, u32[]{:S(2)}, u32[]{:S(2)}) async-start(bf16[16,32,2048]{2,1,0:T(8,128)(2,1)} %broadcast_in_dim.113), calls=%async_computation | async-start | bytes 4194304 | tf_op jit(solution)/shard_map/all_to_all | solution.py:14
  56.4 14.3 %copy-start = (bf16[512,512]{1,0:T(8,128)(2,1)}, bf16[512,512]{1,0:T(8,128)(2,1)S(1)}, u32[]{:S(2)}) copy-start(bf16[512,512]{1,0:T(8,128)(2,1)S(1)} %get-tuple-element.43) | copy-start | bytes 1572868
  57.8 23.7 %all-to-all-start.1 = ((bf16[16,1,136,128]{3,2,1,0:T(8,128)(2,1)}), bf16[16,1,136,128]{3,2,1,0:T(8,128)(2,1)S(1)}, u32[]{:S(2)}, u32[]{:S(2)}) async-start(bf16[16,1,136,128]{3,2,1,0:T(8,128)(2,1)} %broadcast_in_dim.122), calls=%async_computation.1 | async-start | bytes 1114112 | tf_op jit(solution)/shard_map/all_to_all | solution.py:14
  65.6 10.8 %collective-permute-start.3 = (bf16[8,128,128]{2,1,0:T(8,128)(2,1)S(1)}, bf16[8,128,128]{2,1,0:T(8,128)(2,1)S(1)}, u32[]{:S(2)}, u32[]{:S(2)}) collective-permute-start(bf16[8,128,128]{2,1,0:T(8,128)(2,1)S(1)} %constant_dynamic-slice_fusion), channel_id=1, source_target_pairs={{0,2},{1,3},{2,0},{3,1},{4,6},{5,7},{6,4},{7,5},{8,10},{9,11},{10,... | collective-permute-start | bytes 786440 | tf_op jit(solution)/shard_map/ppermute | solution.py:133
  67.1 13.4 %collective-permute-start.4 = (bf16[8,128,128]{2,1,0:T(8,128)(2,1)S(1)}, bf16[8,128,128]{2,1,0:T(8,128)(2,1)S(1)}, u32[]{:S(2)}, u32[]{:S(2)}) collective-permute-start(bf16[8,128,128]{2,1,0:T(8,128)(2,1)S(1)} %constant_dynamic-slice_fusion), channel_id=1, source_target_pairs={{0,1},{1,2},{2,3},{3,0},{4,5},{5,6},{6,7},{7,4},{8,9},{9,10},{10,1... | collective-permute-start | bytes 786440 | tf_op jit(solution)/shard_map/ppermute | solution.py:133
  69.5 11.8 %collective-permute-start.5 = (bf16[8,128,128]{2,1,0:T(8,128)(2,1)S(1)}, bf16[8,128,128]{2,1,0:T(8,128)(2,1)S(1)}, u32[]{:S(2)}, u32[]{:S(2)}) collective-permute-start(bf16[8,128,128]{2,1,0:T(8,128)(2,1)S(1)} %constant_dynamic-slice_fusion), channel_id=1, source_target_pairs={{0,3},{1,0},{2,1},{3,2},{4,7},{5,4},{6,5},{7,6},{8,11},{9,8},{10,9... | collective-permute-start | bytes 786440 | tf_op jit(solution)/shard_map/ppermute | solution.py:133
  81.3 7.5 %collective-permute-start.6 = (bf16[3,8,128,128]{3,2,0,1:T(8,128)(2,1)S(1)}, bf16[3,8,128,128]{3,2,0,1:T(8,128)(2,1)S(1)}, u32[]{:S(2)}, u32[]{:S(2)}) collective-permute-start(bf16[3,8,128,128]{3,2,0,1:T(8,128)(2,1)S(1)} %pad_maximum_fusion), channel_id=1, source_target_pairs={{0,16},{16,0},{32,48},{48,32},{64,80},{80,64},{96,112},{112,96},{1... | collective-permute-start | bytes 2359304 | tf_op jit(solution)/shard_map/ppermute | solution.py:135
  85.0 5.5 %collective-permute-start = (bf16[4,32,128]{2,1,0:T(8,128)(2,1)S(1)}, bf16[4,32,128]{2,1,0:T(8,128)(2,1)S(1)}, u32[]{:S(2)}, u32[]{:S(2)}) collective-permute-start(bf16[4,32,128]{2,1,0:T(8,128)(2,1)S(1)} %get-tuple-element.42), channel_id=1, source_target_pairs={{0,2},{1,3},{2,0},{3,1},{4,6},{5,7},{6,4},{7,5},{8,10},{9,11},{10,... | collective-permute-start | bytes 98312 | tf_op jit(solution)/shard_map/ppermute | solution.py:132
  86.9 3.9 %collective-permute-start.1 = (bf16[4,32,128]{2,1,0:T(8,128)(2,1)S(1)}, bf16[4,32,128]{2,1,0:T(8,128)(2,1)S(1)}, u32[]{:S(2)}, u32[]{:S(2)}) collective-permute-start(bf16[4,32,128]{2,1,0:T(8,128)(2,1)S(1)} %get-tuple-element.41), channel_id=1, source_target_pairs={{0,1},{1,2},{2,3},{3,0},{4,5},{5,6},{6,7},{7,4},{8,9},{9,10},{10,1... | collective-permute-start | bytes 98312 | tf_op jit(solution)/shard_map/ppermute | solution.py:132
  88.7 5.1 %collective-permute-start.2 = (bf16[4,32,128]{2,1,0:T(8,128)(2,1)S(1)}, bf16[4,32,128]{2,1,0:T(8,128)(2,1)S(1)}, u32[]{:S(2)}, u32[]{:S(2)}) collective-permute-start(bf16[4,32,128]{2,1,0:T(8,128)(2,1)S(1)} %get-tuple-element.40), channel_id=1, source_target_pairs={{0,3},{1,0},{2,1},{3,2},{4,7},{5,4},{6,5},{7,6},{8,11},{9,8},{10,9... | collective-permute-start | bytes 98312 | tf_op jit(solution)/shard_map/ppermute | solution.py:132
  94.4 7.3 %collective-permute-start.7 = (bf16[32,2048]{1,0:T(8,128)(2,1)S(1)}, bf16[32,2048]{1,0:T(8,128)(2,1)S(1)}, u32[]{:S(2)}, u32[]{:S(2)}) collective-permute-start(bf16[32,2048]{1,0:T(8,128)(2,1)S(1)} %get-tuple-element.25), channel_id=1, source_target_pairs={{0,8},{1,9},{2,10},{3,11},{4,12},{5,13},{6,14},{7,15},{8,0},{9,1},... | collective-permute-start | bytes 393224 | tf_op jit(solution)/shard_map/ppermute | solution.py:151
  96.6 6.5 %collective-permute-start.8 = (bf16[32,2048]{1,0:T(8,128)(2,1)S(1)}, bf16[32,2048]{1,0:T(8,128)(2,1)S(1)}, u32[]{:S(2)}, u32[]{:S(2)}) collective-permute-start(bf16[32,2048]{1,0:T(8,128)(2,1)S(1)} %get-tuple-element.36), channel_id=1, source_target_pairs={{0,4},{1,5},{2,6},{3,7},{4,8},{5,9},{6,10},{7,11},{8,12},{9,13},{1... | collective-permute-start | bytes 393224 | tf_op jit(solution)/shard_map/ppermute | solution.py:151
  97.2 5.9 %collective-permute-start.9 = (bf16[32,2048]{1,0:T(8,128)(2,1)S(1)}, bf16[32,2048]{1,0:T(8,128)(2,1)S(1)}, u32[]{:S(2)}, u32[]{:S(2)}) collective-permute-start(bf16[32,2048]{1,0:T(8,128)(2,1)S(1)} %get-tuple-element.26), channel_id=1, source_target_pairs={{0,12},{1,13},{2,14},{3,15},{4,0},{5,1},{6,2},{7,3},{8,4},{9,5},{1... | collective-permute-start | bytes 393224 | tf_op jit(solution)/shard_map/ppermute | solution.py:151
Sparse Core Ops, SparseCore 0:
  9.2 43.3 all-gather.1
where the time goes:
time: 111 us
  waiting for transfers between devices  47.6 us (43%)
  starting transfers between devices  24.9 us (22%)
  between operations  17.6 us (16%)
  matrix products  7.4 us (7%)
  local copies, waits for them, and re-layouts  7.38 us (7%)
  other arithmetic  5.77 us (5%)
    all_to_all x2, waiting for transfers between devices, gather_by_exchange(): return lax.all_to_all(copies, axis, 0, 0, tiled=False)  22.9 us
    all_to_all x2, starting transfers between devices, gather_by_exchange(): return lax.all_to_all(copies, axis, 0, 0, tiled=False)  11.6 us
    ppermute x3, waiting for transfers between devices, shards(): fetched.append(lax.ppermute(own_half, 'head', across))  10.5 us
    all_gather x1, waiting for transfers between devices, shards(): stacked = lax.all_gather(packed, 'tm', axis=0, tiled=True)  6.14 us
    ppermute x3, starting transfers between devices, shards(): total = total + lax.ppermute(piece, 'head', down).astype(jnp.float32)  5.39 us
    ppermute x3, waiting for transfers between devices, shards(): pieces.append(lax.ppermute(piece, 'head', across))  4.76 us
    ppermute x3, starting transfers between devices, shards(): pieces.append(lax.ppermute(piece, 'head', across))  3.92 us
    ppermute x3, starting transfers between devices, shards(): fetched.append(lax.ppermute(own_half, 'head', across))  3.91 us
  transfers between devices with their start and end apart: 13, of which 10 were waited for; matrix products, arithmetic and copies ran while one was open for 11% of the time, Pallas kernels for 0%

commit v1 on v0

--- a/solution.py
+++ b/solution.py
@@ -50,7 +50,12 @@
     for start, block in reversed(list(zip(range(0, width, head_width), blocks))[:-1]):
         padded = jnp.pad(block, ((0, 0), (start, width - start - head_width)))
         packed = jnp.where(column < start + head_width, padded, packed)
-    stacked = lax.all_gather(packed, "tm", axis=0, tiled=True)
+    ring = [packed]
+    for hop in range(15):
+        ring.append(lax.ppermute(ring[-1], "tm", [(dev, (dev + 1) % 16) for dev in range(16)]))
+    stacked = jnp.roll(
+        jnp.concatenate(ring[::-1], axis=0), (lax.axis_index("tm") + 1) * ring[0].shape[0], axis=0
+    )
     joined = stacked[:, : 4 * head_width]
     out_blocks = stacked[:, 4 * head_width :].reshape(-1, head_width, w_out.shape[1])
     frames_here = gather_by_exchange(frames, "head").reshape(-1, frames.shape[1])

time: 111 us -> 187 us (1.68)
  waiting for transfers between devices: 47.6 us -> 99.4 us
  local copies, waits for them, and re-layouts: 7.38 us -> 41.9 us
  between operations: 17.6 us -> 4.22 us
  starting transfers between devices: 24.9 us -> 27.3 us
    ppermute x0 -> x15, waiting for transfers between devices: none -> 82.3 us  [shards(): lax.ppermute(ring[-1], 'tm', [(dev, (dev + 1) % 16) for dev in range(16)])]
    unnamed x4 -> x51, local copies, waits for them, and re-layouts: 0.01 us -> 33.7 us
    all_to_all x2, waiting for transfers between devices: 22.9 us -> 0.01 us  [gather_by_exchange(): return lax.all_to_all(copies, axis, 0, 0, tiled=False)]
    all_gather x1 -> x0, waiting for transfers between devices: 6.14 us -> none  [shards(): stacked = lax.all_gather(packed, 'tm', axis=0, tiled=True)]
    all_to_all x2, starting transfers between devices: 11.6 us -> 13.6 us  [gather_by_exchange(): return lax.all_to_all(copies, axis, 0, 0, tiled=False)]
  transfers between devices with their start and end apart: 13 -> 27, of which waited for: 10 -> 21; matrix products, arithmetic and copies ran while one was open for 11% -> 24% of each run, Pallas kernels for 0% -> 0%
where the time goes in v1:
time: 187 us; the launch traced here: 186 us
  waiting for transfers between devices  99.4 us (53%)
  local copies, waits for them, and re-layouts  41.9 us (22%)
  starting transfers between devices  27.3 us (15%)
  matrix products  8.46 us (5%)
  other arithmetic  5.04 us (3%)
  between operations  4.22 us (2%)
    ppermute x15, waiting for transfers between devices, shards(): lax.ppermute(ring[-1], 'tm', [(dev, (dev + 1) % 16) for dev in range(16)])  82.3 us
    unnamed x51, local copies, waits for them, and re-layouts  33.7 us
    all_to_all x2, starting transfers between devices, gather_by_exchange(): return lax.all_to_all(copies, axis, 0, 0, tiled=False)  13.6 us
    ppermute x3, waiting for transfers between devices, shards(): fetched.append(lax.ppermute(own_half, 'head', across))  9.78 us
    ppermute x3, starting transfers between devices, shards(): total = total + lax.ppermute(piece, 'head', down).astype(jnp.float32)  6.3 us
    ppermute x3, waiting for transfers between devices, shards(): pieces.append(lax.ppermute(piece, 'head', across))  4.12 us
    dot_general x1, matrix products, shards(): projected = jnp.dot(frames_here, joined, preferred_element_type=jnp.float32)  3.85 us
  transfers between devices with their start and end apart: 27, of which 21 were waited for; matrix products, arithmetic and copies ran while one was open for 24% of the time, Pallas kernels for 0%

profile of v1, /device:TPU:6, one launch (start us, length us, event | category | flops | bytes accessed | tf_op | source)
XLA Modules:
  0.0 186.3 jit_solution(2089214980598497506)
XLA Ops:
  0.0 0.9 select_select_fusion
  0.9 8.3 %collective-permute-done = bf16[128,640]{1,0:T(8,128)(2,1)S(1)} collective-permute-done((bf16[128,640]{1,0:T(8,128)(2,1)S(1)}, bf16[128,640]{1,0:T(8,128)(2,1)S(1)}, u32[]{:S(2)}, u32[]{:S(2)}) %collective-permute-start) | collective-permute-done | bytes 163872 | tf_op jit(solution)/shard_map/ppermute | solution.py:55
  9.2 6.0 %collective-permute-done.1 = bf16[128,640]{1,0:T(8,128)(2,1)S(1)} collective-permute-done((bf16[128,640]{1,0:T(8,128)(2,1)S(1)}, bf16[128,640]{1,0:T(8,128)(2,1)S(1)}, u32[]{:S(2)}, u32[]{:S(2)}) %collective-permute-start.1) | collective-permute-done | bytes 163872 | tf_op jit(solution)/shard_map/ppermute | solution.py:55
  15.2 6.0 %collective-permute-done.2 = bf16[128,640]{1,0:T(8,128)(2,1)S(1)} collective-permute-done((bf16[128,640]{1,0:T(8,128)(2,1)S(1)}, bf16[128,640]{1,0:T(8,128)(2,1)S(1)}, u32[]{:S(2)}, u32[]{:S(2)}) %collective-permute-start.2) | collective-permute-done | bytes 163872 | tf_op jit(solution)/shard_map/ppermute | solution.py:55
  21.1 6.0 %collective-permute-done.3 = bf16[128,640]{1,0:T(8,128)(2,1)S(1)} collective-permute-done((bf16[128,640]{1,0:T(8,128)(2,1)S(1)}, bf16[128,640]{1,0:T(8,128)(2,1)S(1)}, u32[]{:S(2)}, u32[]{:S(2)}) %collective-permute-start.3) | collective-permute-done | bytes 163872 | tf_op jit(solution)/shard_map/ppermute | solution.py:55
  27.1 6.0 %collective-permute-done.4 = bf16[128,640]{1,0:T(8,128)(2,1)S(1)} collective-permute-done((bf16[128,640]{1,0:T(8,128)(2,1)S(1)}, bf16[128,640]{1,0:T(8,128)(2,1)S(1)}, u32[]{:S(2)}, u32[]{:S(2)}) %collective-permute-start.4) | collective-permute-done | bytes 163872 | tf_op jit(solution)/shard_map/ppermute | solution.py:55
  33.0 6.0 %collective-permute-done.5 = bf16[128,640]{1,0:T(8,128)(2,1)S(1)} collective-permute-done((bf16[128,640]{1,0:T(8,128)(2,1)S(1)}, bf16[128,640]{1,0:T(8,128)(2,1)S(1)}, u32[]{:S(2)}, u32[]{:S(2)}) %collective-permute-start.5) | collective-permute-done | bytes 163872 | tf_op jit(solution)/shard_map/ppermute | solution.py:55
  39.0 6.0 %collective-permute-done.6 = bf16[128,640]{1,0:T(8,128)(2,1)S(1)} collective-permute-done((bf16[128,640]{1,0:T(8,128)(2,1)S(1)}, bf16[128,640]{1,0:T(8,128)(2,1)S(1)}, u32[]{:S(2)}, u32[]{:S(2)}) %collective-permute-start.6) | collective-permute-done | bytes 163872 | tf_op jit(solution)/shard_map/ppermute | solution.py:55
  45.0 6.0 %collective-permute-done.7 = bf16[128,640]{1,0:T(8,128)(2,1)S(1)} collective-permute-done((bf16[128,640]{1,0:T(8,128)(2,1)S(1)}, bf16[128,640]{1,0:T(8,128)(2,1)S(1)}, u32[]{:S(2)}, u32[]{:S(2)}) %collective-permute-start.7) | collective-permute-done | bytes 163872 | tf_op jit(solution)/shard_map/ppermute | solution.py:55
  51.6 6.0 %collective-permute-done.8 = bf16[128,640]{1,0:T(8,128)(2,1)S(1)} collective-permute-done((bf16[128,640]{1,0:T(8,128)(2,1)S(1)}, bf16[128,640]{1,0:T(8,128)(2,1)S(1)}, u32[]{:S(2)}, u32[]{:S(2)}) %collective-permute-start.8) | collective-permute-done | bytes 163872 | tf_op jit(solution)/shard_map/ppermute | solution.py:55
  58.2 6.0 %collective-permute-done.9 = bf16[128,640]{1,0:T(8,128)(2,1)S(1)} collective-permute-done((bf16[128,640]{1,0:T(8,128)(2,1)S(1)}, bf16[128,640]{1,0:T(8,128)(2,1)S(1)}, u32[]{:S(2)}, u32[]{:S(2)}) %collective-permute-start.9) | collective-permute-done | bytes 163872 | tf_op jit(solution)/shard_map/ppermute | solution.py:55
  64.8 6.0 %collective-permute-done.10 = bf16[128,640]{1,0:T(8,128)(2,1)S(1)} collective-permute-done((bf16[128,640]{1,0:T(8,128)(2,1)S(1)}, bf16[128,640]{1,0:T(8,128)(2,1)S(1)}, u32[]{:S(2)}, u32[]{:S(2)}) %collective-permute-start.10) | collective-permute-done | bytes 163872 | tf_op jit(solution)/shard_map/ppermute | solution.py:55
  71.4 6.1 %collective-permute-done.11 = bf16[128,640]{1,0:T(8,128)(2,1)} collective-permute-done((bf16[128,640]{1,0:T(8,128)(2,1)S(1)}, bf16[128,640]{1,0:T(8,128)(2,1)}, u32[]{:S(2)}, u32[]{:S(2)}) %collective-permute-start.11) | collective-permute-done | bytes 163872 | tf_op jit(solution)/shard_map/ppermute | solution.py:55
  77.5 2.5 %broadcast_in_dim.113 = bf16[16,32,2048]{2,1,0:T(8,128)(2,1)} broadcast(bf16[32,2048]{1,0:T(8,128)(2,1)} %param.7), dimensions={1,2} | broadcast | bytes 2228224 | tf_op jit(solution)/shard_map/broadcast_in_dim | solution.py:13
  80.0 7.4 %all-to-all-start = ((bf16[16,32,2048]{2,1,0:T(8,128)(2,1)}), bf16[16,32,2048]{2,1,0:T(8,128)(2,1)S(1)}, u32[]{:S(2)}, u32[]{:S(2)}) async-start(bf16[16,32,2048]{2,1,0:T(8,128)(2,1)} %broadcast_in_dim.113), calls=%async_computation | async-start | bytes 4194304 | tf_op jit(solution)/shard_map/all_to_all | solution.py:14
  92.6 2.4 %collective-permute-done.13 = bf16[128,640]{1,0:T(8,128)(2,1)} collective-permute-done((bf16[128,640]{1,0:T(8,128)(2,1)}, bf16[128,640]{1,0:T(8,128)(2,1)}, u32[]{:S(2)}, u32[]{:S(2)}) %collective-permute-start.13) | collective-permute-done | bytes 163872 | tf_op jit(solution)/shard_map/ppermute | solution.py:55
  95.1 6.1 %collective-permute-done.14 = bf16[128,640]{1,0:T(8,128)(2,1)S(1)} collective-permute-done((bf16[128,640]{1,0:T(8,128)(2,1)}, bf16[128,640]{1,0:T(8,128)(2,1)S(1)}, u32[]{:S(2)}, u32[]{:S(2)}) %collective-permute-start.14) | collective-permute-done | bytes 163872 | tf_op jit(solution)/shard_map/ppermute | solution.py:55
  101.8 1.6 constant_dynamic-update-slice_fusion.30
  103.4 1.6 constant_dynamic-update-slice_fusion.29
  105.0 1.6 constant_dynamic-update-slice_fusion.28
  106.6 1.6 constant_dynamic-update-slice_fusion.27
  108.2 1.6 constant_dynamic-update-slice_fusion.26
  109.8 1.6 constant_dynamic-update-slice_fusion.25
  111.4 1.6 constant_dynamic-update-slice_fusion.24
  119.1 1.6 constant_dynamic-update-slice_fusion.14
  120.7 1.6 constant_dynamic-update-slice_fusion.13
  122.3 1.6 constant_dynamic-update-slice_fusion.12
  132.1 3.9 %fusion.59 = (bf16[512,512]{1,0:T(8,128)(2,1)S(1)}, f32[512,512]{1,0:T(8,128)}) fusion(bf16[512,2048]{1,0:T(8,128)(2,1)S(1)} %bitcast.110, bf16[4096,640]{1,0:T(8,128)(2,1)} %constant_dynamic-update-slice_fusion, s32[]{:T(128)S(6)} %select_n.138), kind=kOutput, calls=%fused_computation.128 | convolution fusion | flops 1074003968 | bytes 5767172 | tf_op jit(solution)/shard_map/dot_general | solution.py:62
  137.2 0.9 broadcast_in_dim.122
  138.1 6.2 %all-to-all-start.1 = ((bf16[16,1,136,128]{3,2,1,0:T(8,128)(2,1)}), bf16[16,1,136,128]{3,2,1,0:T(8,128)(2,1)S(1)}, u32[]{:S(2)}, u32[]{:S(2)}) async-start(bf16[16,1,136,128]{3,2,1,0:T(8,128)(2,1)} %broadcast_in_dim.122), calls=%async_computation.1 | async-start | bytes 1114112 | tf_op jit(solution)/shard_map/all_to_all | solution.py:14
  147.1 1.1 dynamic-slice.1
  148.3 1.5 collective-permute-start.18
  149.8 2.1 %collective-permute-start.19 = (bf16[8,128,128]{2,1,0:T(8,128)(2,1)S(1)}, bf16[8,128,128]{2,1,0:T(8,128)(2,1)S(1)}, u32[]{:S(2)}, u32[]{:S(2)}) collective-permute-start(bf16[8,128,128]{2,1,0:T(8,128)(2,1)S(1)} %constant_dynamic-slice_fusion), channel_id=1, source_target_pairs={{0,1},{1,2},{2,3},{3,0},{4,5},{5,6},{6,7},{7,4},{8,9},{9,10},{10,1... | collective-permute-start | bytes 786440 | tf_op jit(solution)/shard_map/ppermute | solution.py:138
  151.9 2.3 %fusion.15 = f32[1,512,1,128]{3,1,2,0:T(8,128)} fusion(f32[512]{0:T(512)S(1)} %get-tuple-element.22, bf16[512,512]{1,0:T(8,128)(2,1)} %copy-done.8), kind=kOutput, calls=%fused_computation.16 | convolution fusion | flops 135528448 | bytes 659456 | tf_op jit(solution)/shard_map/while/body/eval_jaxpr/hts,shd->thd/dot_general | solution.py:94
  154.2 4.9 %collective-permute-done.18 = bf16[8,128,128]{2,1,0:T(8,128)(2,1)S(1)} collective-permute-done((bf16[8,128,128]{2,1,0:T(8,128)(2,1)S(1)}, bf16[8,128,128]{2,1,0:T(8,128)(2,1)S(1)}, u32[]{:S(2)}, u32[]{:S(2)}) %collective-permute-start.18) | collective-permute-done | bytes 262176 | tf_op jit(solution)/shard_map/ppermute | solution.py:138
  159.0 2.6 %collective-permute-done.19 = bf16[8,128,128]{2,1,0:T(8,128)(2,1)S(1)} collective-permute-done((bf16[8,128,128]{2,1,0:T(8,128)(2,1)S(1)}, bf16[8,128,128]{2,1,0:T(8,128)(2,1)S(1)}, u32[]{:S(2)}, u32[]{:S(2)}) %collective-permute-start.19) | collective-permute-done | bytes 262176 | tf_op jit(solution)/shard_map/ppermute | solution.py:138
  161.6 2.3 %collective-permute-done.20 = bf16[8,128,128]{2,1,0:T(8,128)(2,1)S(1)} collective-permute-done((bf16[8,128,128]{2,1,0:T(8,128)(2,1)S(1)}, bf16[8,128,128]{2,1,0:T(8,128)(2,1)S(1)}, u32[]{:S(2)}, u32[]{:S(2)}) %collective-permute-start.20) | collective-permute-done | bytes 262176 | tf_op jit(solution)/shard_map/ppermute | solution.py:138
  164.7 1.5 fusion.60
  166.5 1.2 fusion.32
  167.6 1.6 collective-permute-start.15
  169.2 1.2 collective-permute-start.16
  170.4 0.9 collective-permute-start.17
  171.4 1.7 collective-permute-done.15
  173.2 2.4 %collective-permute-done.17 = bf16[4,32,128]{2,1,0:T(8,128)(2,1)S(1)} collective-permute-done((bf16[4,32,128]{2,1,0:T(8,128)(2,1)S(1)}, bf16[4,32,128]{2,1,0:T(8,128)(2,1)S(1)}, u32[]{:S(2)}, u32[]{:S(2)}) %collective-permute-start.17) | collective-permute-done | bytes 32800 | tf_op jit(solution)/shard_map/ppermute | solution.py:137
  176.2 3.1 %collective-permute-start.22 = (bf16[32,2048]{1,0:T(8,128)(2,1)S(1)}, bf16[32,2048]{1,0:T(8,128)(2,1)S(1)}, u32[]{:S(2)}, u32[]{:S(2)}) collective-permute-start(bf16[32,2048]{1,0:T(8,128)(2,1)S(1)} %get-tuple-element.25), channel_id=1, source_target_pairs={{0,8},{1,9},{2,10},{3,11},{4,12},{5,13},{6,14},{7,15},{8,0},{9,1},... | collective-permute-start | bytes 393224 | tf_op jit(solution)/shard_map/ppermute | solution.py:156
  179.8 2.7 %collective-permute-start.24 = (bf16[32,2048]{1,0:T(8,128)(2,1)S(1)}, bf16[32,2048]{1,0:T(8,128)(2,1)S(1)}, u32[]{:S(2)}, u32[]{:S(2)}) collective-permute-start(bf16[32,2048]{1,0:T(8,128)(2,1)S(1)} %get-tuple-element.26), channel_id=1, source_target_pairs={{0,12},{1,13},{2,14},{3,15},{4,0},{5,1},{6,2},{7,3},{8,4},{9,5},{1... | collective-permute-start | bytes 393224 | tf_op jit(solution)/shard_map/ppermute | solution.py:156
  182.5 1.4 collective-permute-done.22
  183.8 1.8 collective-permute-done.23
  (102 shorter events, 26.0 us)
Async XLA Ops:
  0.0 87.4 %copy-start.9 = (f32[512,1]{0,1:T(1,128)S(1)}, f32[512,1]{0,1:T(1,128)}, u32[]{:S(2)}) copy-start(f32[512,1]{0,1:T(1,128)} %param.8) | copy-start | bytes 6148
  0.9 8.3 %collective-permute-start = (bf16[128,640]{1,0:T(8,128)(2,1)S(1)}, bf16[128,640]{1,0:T(8,128)(2,1)S(1)}, u32[]{:S(2)}, u32[]{:S(2)}) collective-permute-start(bf16[128,640]{1,0:T(8,128)(2,1)S(1)} %select_select_fusion), channel_id=1, source_target_pairs={{0,16},{16,32},{32,48},{48,64},{64,80},{80,96},{96,112},{112,128},... | collective-permute-start | bytes 491528 | tf_op jit(solution)/shard_map/ppermute | solution.py:55
  9.2 6.0 %collective-permute-start.1 = (bf16[128,640]{1,0:T(8,128)(2,1)S(1)}, bf16[128,640]{1,0:T(8,128)(2,1)S(1)}, u32[]{:S(2)}, u32[]{:S(2)}) collective-permute-start(bf16[128,640]{1,0:T(8,128)(2,1)S(1)} %collective-permute-done), channel_id=1, source_target_pairs={{0,16},{16,32},{32,48},{48,64},{64,80},{80,96},{96,112},{112,128},... | collective-permute-start | bytes 491528 | tf_op jit(solution)/shard_map/ppermute | solution.py:55
  15.2 6.0 %collective-permute-start.2 = (bf16[128,640]{1,0:T(8,128)(2,1)S(1)}, bf16[128,640]{1,0:T(8,128)(2,1)S(1)}, u32[]{:S(2)}, u32[]{:S(2)}) collective-permute-start(bf16[128,640]{1,0:T(8,128)(2,1)S(1)} %collective-permute-done.1), channel_id=1, source_target_pairs={{0,16},{16,32},{32,48},{48,64},{64,80},{80,96},{96,112},{112,128},... | collective-permute-start | bytes 491528 | tf_op jit(solution)/shard_map/ppermute | solution.py:55
  21.1 6.0 %collective-permute-start.3 = (bf16[128,640]{1,0:T(8,128)(2,1)S(1)}, bf16[128,640]{1,0:T(8,128)(2,1)S(1)}, u32[]{:S(2)}, u32[]{:S(2)}) collective-permute-start(bf16[128,640]{1,0:T(8,128)(2,1)S(1)} %collective-permute-done.2), channel_id=1, source_target_pairs={{0,16},{16,32},{32,48},{48,64},{64,80},{80,96},{96,112},{112,128},... | collective-permute-start | bytes 491528 | tf_op jit(solution)/shard_map/ppermute | solution.py:55
  27.1 6.0 %collective-permute-start.4 = (bf16[128,640]{1,0:T(8,128)(2,1)S(1)}, bf16[128,640]{1,0:T(8,128)(2,1)S(1)}, u32[]{:S(2)}, u32[]{:S(2)}) collective-permute-start(bf16[128,640]{1,0:T(8,128)(2,1)S(1)} %collective-permute-done.3), channel_id=1, source_target_pairs={{0,16},{16,32},{32,48},{48,64},{64,80},{80,96},{96,112},{112,128},... | collective-permute-start | bytes 491528 | tf_op jit(solution)/shard_map/ppermute | solution.py:55
  33.0 6.0 %collective-permute-start.5 = (bf16[128,640]{1,0:T(8,128)(2,1)S(1)}, bf16[128,640]{1,0:T(8,128)(2,1)S(1)}, u32[]{:S(2)}, u32[]{:S(2)}) collective-permute-start(bf16[128,640]{1,0:T(8,128)(2,1)S(1)} %collective-permute-done.4), channel_id=1, source_target_pairs={{0,16},{16,32},{32,48},{48,64},{64,80},{80,96},{96,112},{112,128},... | collective-permute-start | bytes 491528 | tf_op jit(solution)/shard_map/ppermute | solution.py:55
  39.0 6.0 %collective-permute-start.6 = (bf16[128,640]{1,0:T(8,128)(2,1)S(1)}, bf16[128,640]{1,0:T(8,128)(2,1)S(1)}, u32[]{:S(2)}, u32[]{:S(2)}) collective-permute-start(bf16[128,640]{1,0:T(8,128)(2,1)S(1)} %collective-permute-done.5), channel_id=1, source_target_pairs={{0,16},{16,32},{32,48},{48,64},{64,80},{80,96},{96,112},{112,128},... | collective-permute-start | bytes 491528 | tf_op jit(solution)/shard_map/ppermute | solution.py:55
  45.0 6.0 %collective-permute-start.7 = (bf16[128,640]{1,0:T(8,128)(2,1)S(1)}, bf16[128,640]{1,0:T(8,128)(2,1)S(1)}, u32[]{:S(2)}, u32[]{:S(2)}) collective-permute-start(bf16[128,640]{1,0:T(8,128)(2,1)S(1)} %collective-permute-done.6), channel_id=1, source_target_pairs={{0,16},{16,32},{32,48},{48,64},{64,80},{80,96},{96,112},{112,128},... | collective-permute-start | bytes 491528 | tf_op jit(solution)/shard_map/ppermute | solution.py:55
  50.9 0.7 copy-start
  51.6 6.0 %collective-permute-start.8 = (bf16[128,640]{1,0:T(8,128)(2,1)S(1)}, bf16[128,640]{1,0:T(8,128)(2,1)S(1)}, u32[]{:S(2)}, u32[]{:S(2)}) collective-permute-start(bf16[128,640]{1,0:T(8,128)(2,1)S(1)} %collective-permute-done.7), channel_id=1, source_target_pairs={{0,16},{16,32},{32,48},{48,64},{64,80},{80,96},{96,112},{112,128},... | collective-permute-start | bytes 491528 | tf_op jit(solution)/shard_map/ppermute | solution.py:55
  57.5 0.7 copy-start.2
  58.2 6.0 %collective-permute-start.9 = (bf16[128,640]{1,0:T(8,128)(2,1)S(1)}, bf16[128,640]{1,0:T(8,128)(2,1)S(1)}, u32[]{:S(2)}, u32[]{:S(2)}) collective-permute-start(bf16[128,640]{1,0:T(8,128)(2,1)S(1)} %collective-permute-done.8), channel_id=1, source_target_pairs={{0,16},{16,32},{32,48},{48,64},{64,80},{80,96},{96,112},{112,128},... | collective-permute-start | bytes 491528 | tf_op jit(solution)/shard_map/ppermute | solution.py:55
  64.1 0.7 copy-start.4
  64.8 6.0 %collective-permute-start.10 = (bf16[128,640]{1,0:T(8,128)(2,1)S(1)}, bf16[128,640]{1,0:T(8,128)(2,1)S(1)}, u32[]{:S(2)}, u32[]{:S(2)}) collective-permute-start(bf16[128,640]{1,0:T(8,128)(2,1)S(1)} %collective-permute-done.9), channel_id=1, source_target_pairs={{0,16},{16,32},{32,48},{48,64},{64,80},{80,96},{96,112},{112,128},... | collective-permute-start | bytes 491528 | tf_op jit(solution)/shard_map/ppermute | solution.py:55
  70.8 0.7 copy-start.6
  71.4 6.1 %collective-permute-start.11 = (bf16[128,640]{1,0:T(8,128)(2,1)S(1)}, bf16[128,640]{1,0:T(8,128)(2,1)}, u32[]{:S(2)}, u32[]{:S(2)}) collective-permute-start(bf16[128,640]{1,0:T(8,128)(2,1)S(1)} %collective-permute-done.10), channel_id=1, source_target_pairs={{0,16},{16,32},{32,48},{48,64},{64,80},{80,96},{96,112},{112,128},... | collective-permute-start | bytes 491528 | tf_op jit(solution)/shard_map/ppermute | solution.py:55
  77.5 11.2 %collective-permute-start.12 = (bf16[128,640]{1,0:T(8,128)(2,1)}, bf16[128,640]{1,0:T(8,128)(2,1)}, u32[]{:S(2)}, u32[]{:S(2)}) collective-permute-start(bf16[128,640]{1,0:T(8,128)(2,1)} %collective-permute-done.11), channel_id=1, source_target_pairs={{0,16},{16,32},{32,48},{48,64},{64,80},{80,96},{96,112},{112,128},... | collective-permute-start | bytes 491528 | tf_op jit(solution)/shard_map/ppermute | solution.py:55
  80.0 52.1 %all-to-all-start = ((bf16[16,32,2048]{2,1,0:T(8,128)(2,1)}), bf16[16,32,2048]{2,1,0:T(8,128)(2,1)S(1)}, u32[]{:S(2)}, u32[]{:S(2)}) async-start(bf16[16,32,2048]{2,1,0:T(8,128)(2,1)} %broadcast_in_dim.113), calls=%async_computation | async-start | bytes 4194304 | tf_op jit(solution)/shard_map/all_to_all | solution.py:14
  88.7 6.3 %collective-permute-start.13 = (bf16[128,640]{1,0:T(8,128)(2,1)}, bf16[128,640]{1,0:T(8,128)(2,1)}, u32[]{:S(2)}, u32[]{:S(2)}) collective-permute-start(bf16[128,640]{1,0:T(8,128)(2,1)} %collective-permute-done.12), channel_id=1, source_target_pairs={{0,16},{16,32},{32,48},{48,64},{64,80},{80,96},{96,112},{112,128},... | collective-permute-start | bytes 491528 | tf_op jit(solution)/shard_map/ppermute | solution.py:55
  92.6 31.3 %copy-start.7 = (bf16[128,640]{1,0:T(8,128)(2,1)S(1)}, bf16[128,640]{1,0:T(8,128)(2,1)}, u32[]{:S(2)}) copy-start(bf16[128,640]{1,0:T(8,128)(2,1)} %copy-done.6) | copy-start | bytes 491524
  92.6 32.0 %copy-start.5 = (bf16[128,640]{1,0:T(8,128)(2,1)S(1)}, bf16[128,640]{1,0:T(8,128)(2,1)}, u32[]{:S(2)}) copy-start(bf16[128,640]{1,0:T(8,128)(2,1)} %copy-done.4) | copy-start | bytes 491524
  92.6 32.7 %copy-start.3 = (bf16[128,640]{1,0:T(8,128)(2,1)S(1)}, bf16[128,640]{1,0:T(8,128)(2,1)}, u32[]{:S(2)}) copy-start(bf16[128,640]{1,0:T(8,128)(2,1)} %copy-done.2) | copy-start | bytes 491524
  92.6 33.3 %copy-start.1 = (bf16[128,640]{1,0:T(8,128)(2,1)S(1)}, bf16[128,640]{1,0:T(8,128)(2,1)}, u32[]{:S(2)}) copy-start(bf16[128,640]{1,0:T(8,128)(2,1)} %copy-done) | copy-start | bytes 491524
  95.0 6.2 %collective-permute-start.14 = (bf16[128,640]{1,0:T(8,128)(2,1)}, bf16[128,640]{1,0:T(8,128)(2,1)S(1)}, u32[]{:S(2)}, u32[]{:S(2)}) collective-permute-start(bf16[128,640]{1,0:T(8,128)(2,1)} %collective-permute-done.13), channel_id=1, source_target_pairs={{0,16},{16,32},{32,48},{48,64},{64,80},{80,96},{96,112},{112,128},... | collective-permute-start | bytes 491528 | tf_op jit(solution)/shard_map/ppermute | solution.py:55
  135.9 0.8 copy-start.8
  138.1 26.0 %all-to-all-start.1 = ((bf16[16,1,136,128]{3,2,1,0:T(8,128)(2,1)}), bf16[16,1,136,128]{3,2,1,0:T(8,128)(2,1)S(1)}, u32[]{:S(2)}, u32[]{:S(2)}) async-start(bf16[16,1,136,128]{3,2,1,0:T(8,128)(2,1)} %broadcast_in_dim.122), calls=%async_computation.1 | async-start | bytes 1114112 | tf_op jit(solution)/shard_map/all_to_all | solution.py:14
  148.3 10.8 %collective-permute-start.18 = (bf16[8,128,128]{2,1,0:T(8,128)(2,1)S(1)}, bf16[8,128,128]{2,1,0:T(8,128)(2,1)S(1)}, u32[]{:S(2)}, u32[]{:S(2)}) collective-permute-start(bf16[8,128,128]{2,1,0:T(8,128)(2,1)S(1)} %constant_dynamic-slice_fusion), channel_id=1, source_target_pairs={{0,2},{1,3},{2,0},{3,1},{4,6},{5,7},{6,4},{7,5},{8,10},{9,11},{10,... | collective-permute-start | bytes 786440 | tf_op jit(solution)/shard_map/ppermute | solution.py:138
  149.8 11.8 %collective-permute-start.19 = (bf16[8,128,128]{2,1,0:T(8,128)(2,1)S(1)}, bf16[8,128,128]{2,1,0:T(8,128)(2,1)S(1)}, u32[]{:S(2)}, u32[]{:S(2)}) collective-permute-start(bf16[8,128,128]{2,1,0:T(8,128)(2,1)S(1)} %constant_dynamic-slice_fusion), channel_id=1, source_target_pairs={{0,1},{1,2},{2,3},{3,0},{4,5},{5,6},{6,7},{7,4},{8,9},{9,10},{10,1... | collective-permute-start | bytes 786440 | tf_op jit(solution)/shard_map/ppermute | solution.py:138
  151.9 12.1 %collective-permute-start.20 = (bf16[8,128,128]{2,1,0:T(8,128)(2,1)S(1)}, bf16[8,128,128]{2,1,0:T(8,128)(2,1)S(1)}, u32[]{:S(2)}, u32[]{:S(2)}) collective-permute-start(bf16[8,128,128]{2,1,0:T(8,128)(2,1)S(1)} %constant_dynamic-slice_fusion), channel_id=1, source_target_pairs={{0,3},{1,0},{2,1},{3,2},{4,7},{5,4},{6,5},{7,6},{8,11},{9,8},{10,9... | collective-permute-start | bytes 786440 | tf_op jit(solution)/shard_map/ppermute | solution.py:138
  164.0 7.2 %collective-permute-start.21 = (bf16[3,8,128,128]{3,2,0,1:T(8,128)(2,1)S(1)}, bf16[3,8,128,128]{3,2,0,1:T(8,128)(2,1)S(1)}, u32[]{:S(2)}, u32[]{:S(2)}) collective-permute-start(bf16[3,8,128,128]{3,2,0,1:T(8,128)(2,1)S(1)} %pad_maximum_fusion), channel_id=1, source_target_pairs={{0,16},{16,0},{32,48},{48,32},{64,80},{80,64},{96,112},{112,96},{1... | collective-permute-start | bytes 2359304 | tf_op jit(solution)/shard_map/ppermute | solution.py:140
  167.6 5.5 %collective-permute-start.15 = (bf16[4,32,128]{2,1,0:T(8,128)(2,1)S(1)}, bf16[4,32,128]{2,1,0:T(8,128)(2,1)S(1)}, u32[]{:S(2)}, u32[]{:S(2)}) collective-permute-start(bf16[4,32,128]{2,1,0:T(8,128)(2,1)S(1)} %get-tuple-element.42), channel_id=1, source_target_pairs={{0,2},{1,3},{2,0},{3,1},{4,6},{5,7},{6,4},{7,5},{8,10},{9,11},{10,... | collective-permute-start | bytes 98312 | tf_op jit(solution)/shard_map/ppermute | solution.py:137
  169.2 3.9 %collective-permute-start.16 = (bf16[4,32,128]{2,1,0:T(8,128)(2,1)S(1)}, bf16[4,32,128]{2,1,0:T(8,128)(2,1)S(1)}, u32[]{:S(2)}, u32[]{:S(2)}) collective-permute-start(bf16[4,32,128]{2,1,0:T(8,128)(2,1)S(1)} %get-tuple-element.41), channel_id=1, source_target_pairs={{0,1},{1,2},{2,3},{3,0},{4,5},{5,6},{6,7},{7,4},{8,9},{9,10},{10,1... | collective-permute-start | bytes 98312 | tf_op jit(solution)/shard_map/ppermute | solution.py:137
  170.4 5.1 %collective-permute-start.17 = (bf16[4,32,128]{2,1,0:T(8,128)(2,1)S(1)}, bf16[4,32,128]{2,1,0:T(8,128)(2,1)S(1)}, u32[]{:S(2)}, u32[]{:S(2)}) collective-permute-start(bf16[4,32,128]{2,1,0:T(8,128)(2,1)S(1)} %get-tuple-element.40), channel_id=1, source_target_pairs={{0,3},{1,0},{2,1},{3,2},{4,7},{5,4},{6,5},{7,6},{8,11},{9,8},{10,9... | collective-permute-start | bytes 98312 | tf_op jit(solution)/shard_map/ppermute | solution.py:137
  176.2 7.7 %collective-permute-start.22 = (bf16[32,2048]{1,0:T(8,128)(2,1)S(1)}, bf16[32,2048]{1,0:T(8,128)(2,1)S(1)}, u32[]{:S(2)}, u32[]{:S(2)}) collective-permute-start(bf16[32,2048]{1,0:T(8,128)(2,1)S(1)} %get-tuple-element.25), channel_id=1, source_target_pairs={{0,8},{1,9},{2,10},{3,11},{4,12},{5,13},{6,14},{7,15},{8,0},{9,1},... | collective-permute-start | bytes 393224 | tf_op jit(solution)/shard_map/ppermute | solution.py:156
  179.2 6.4 %collective-permute-start.23 = (bf16[32,2048]{1,0:T(8,128)(2,1)S(1)}, bf16[32,2048]{1,0:T(8,128)(2,1)S(1)}, u32[]{:S(2)}, u32[]{:S(2)}) collective-permute-start(bf16[32,2048]{1,0:T(8,128)(2,1)S(1)} %get-tuple-element.36), channel_id=1, source_target_pairs={{0,4},{1,5},{2,6},{3,7},{4,8},{5,9},{6,10},{7,11},{8,12},{9,13},{1... | collective-permute-start | bytes 393224 | tf_op jit(solution)/shard_map/ppermute | solution.py:156
  179.8 5.8 %collective-permute-start.24 = (bf16[32,2048]{1,0:T(8,128)(2,1)S(1)}, bf16[32,2048]{1,0:T(8,128)(2,1)S(1)}, u32[]{:S(2)}, u32[]{:S(2)}) collective-permute-start(bf16[32,2048]{1,0:T(8,128)(2,1)S(1)} %get-tuple-element.26), channel_id=1, source_target_pairs={{0,12},{1,13},{2,14},{3,15},{4,0},{5,1},{6,2},{7,3},{8,4},{9,5},{1... | collective-permute-start | bytes 393224 | tf_op jit(solution)/shard_map/ppermute | solution.py:156
